TPU v7x, 32 devices: a whole 2x2x4 slice. The times are simulated.
32 devices in a mesh: grp: 2 (over y), blk: 8 (over z, x), tch: 2 (over core).
Axes of the slice: x: 2, y: 2, z: 4, core: 2. Of those that a mesh axis runs over, the one named last changes fastest.
Arguments:
- samples: bfloat16 [4, 32, 65536], P('grp', 'blk', 'tch'), parts along dimension 0, may hold values from -6 to 6
- history: bfloat16 [4, 32, 15360], P('grp', 'blk'), parts along dimension 0, may hold values from -6 to 6
- coefficients: float32 [16, 1024], replicated, may hold values from -1.5 to 1.5
- station_of_slot: int32 [32], P('grp'), parts along dimension 0, may hold values from 0 to 15, each once
- station_ok: int32 [32], P('grp'), parts along dimension 0, may hold values from 0 to 1, as said below
Outputs:
- visibilities: bfloat16 [4, 1024, 32, 32], P('grp', ('blk', 'tch')), parts along dimension 0
There are 2 independent parts, one for each index of `grp`. A program takes and returns all parts, laid end to end along the dimension named above; an argument that names none is the same for every part. Nothing has to cross between parts.
Inputs may be any that keep to these rules, and one draw needn't show every extreme that they name: `station_of_slot`: each station stands in exactly one slot. `station_ok`: 2 or 3 stations are flagged.
All inputs are finite; a program needn't handle non-finite values.
Results may differ from a plain program's by a relative error of at most 0.0074.
Values may be sent and summed in bfloat16 or wider, within the bound.
No kernel may reach another device: no remote copies, remote signals or barrier semaphores. Data moves between devices by JAX's collectives and lax.ppermute only.
A program may use at most 64 MiB of HBM per device.

v0:
```python
import math
import jax
import jax.numpy as jnp
from jax import lax
from jax.sharding import PartitionSpec as P

POLS = 2


def shifted(block, axis, distance):
    devices = range(lax.axis_size(axis))
    route = [(i - distance, i) for i in devices if i - distance in devices]
    return lax.ppermute(block, axis, route)


def dft_table(fft_len):
    row_index = lax.broadcasted_iota(jnp.int32, (fft_len, fft_len), 0)
    col_index = lax.broadcasted_iota(jnp.int32, (fft_len, fft_len), 1)
    phase_step = row_index * col_index % fft_len
    angles = phase_step.astype(jnp.float32) * (2.0 * math.pi / fft_len)
    norm_scale = 1.0 / math.sqrt(fft_len)
    cosine = jnp.cos(angles) * norm_scale
    sine_part = jnp.sin(angles) * norm_scale
    upper_half = jnp.concatenate([cosine, -sine_part], axis=1)
    lower_half = jnp.concatenate([sine_part, cosine], axis=1)
    return jnp.concatenate([upper_half, lower_half], axis=0).astype(jnp.bfloat16)


def filter_bank(extended, coefficients, spec_count):
    tap_count, fft_len = coefficients.shape
    blocks = extended.reshape(extended.shape[0], extended.shape[1], -1, fft_len)
    running = jnp.zeros((extended.shape[0], extended.shape[1], spec_count, fft_len), jnp.float32)
    for tap_index in range(tap_count):
        running = running + coefficients[tap_index] * blocks[
            :, :, tap_index : tap_index + spec_count, :
        ].astype(jnp.float32)
    return running.astype(jnp.bfloat16)


def channel_major(filtered, dft_matrix):
    row_count, spec_count, fft_len = (filtered.shape[1], filtered.shape[2], filtered.shape[3])
    flat_rows = jnp.transpose(filtered, (1, 2, 0, 3)).reshape(row_count * spec_count, 2 * fft_len)
    product = jnp.dot(flat_rows, dft_matrix, preferred_element_type=jnp.float32).astype(
        jnp.bfloat16
    )
    product = product.reshape(row_count, spec_count, 2, fft_len)
    return jnp.transpose(product, (3, 0, 2, 1)).reshape(fft_len, row_count * 2 * spec_count)


def reorder_inputs(values, station_of_slot, station_ok):
    station_count = station_of_slot.shape[0]
    input_count = values.shape[1]
    slot_index = (
        jnp.zeros((station_count,), jnp.int32)
        .at[station_of_slot]
        .set(jnp.arange(station_count, dtype=jnp.int32))
    )
    position = jnp.arange(input_count, dtype=jnp.int32)
    source_rows = slot_index[position // POLS] * POLS + position % POLS
    keep_mask = station_ok[position // POLS].astype(values.dtype)
    return jnp.take(values, source_rows, axis=1) * keep_mask[None, :, None]


def rotate_parts(ordered):
    half_cols = ordered.shape[2] // 2
    return jnp.concatenate([-ordered[:, :, half_cols:], ordered[:, :, :half_cols]], axis=2)


def correlate_full(ordered, inverse_count):
    rotated = rotate_parts(ordered)
    real_vis = jnp.einsum("cak,cbk->cab", ordered, ordered, preferred_element_type=jnp.float32)
    imag_vis = jnp.einsum("cak,cbk->cab", ordered, rotated, preferred_element_type=jnp.float32)
    return (jnp.stack([real_vis, imag_vis], axis=0) * inverse_count).astype(jnp.bfloat16)


def local(samples, history, coefficients, station_of_slot, station_ok):
    tap_count, fft_len = coefficients.shape
    row_count = samples.shape[1]
    spec_local = samples.shape[2] // fft_len
    half_count = lax.axis_size("tch")
    block_count = lax.axis_size("blk")
    spec_total = spec_local * half_count
    dft_matrix = dft_table(fft_len)
    tail_block = jnp.concatenate([history, samples], axis=2)[:, :, -(tap_count - 1) * fft_len :]
    earlier = shifted(tail_block, "tch", 1)
    is_first = lax.axis_index("tch") == 0
    earlier = jnp.where(is_first, history, earlier)
    extended = jnp.concatenate([earlier, samples], axis=2)
    by_channel = channel_major(filter_bank(extended, coefficients, spec_local), dft_matrix)
    by_block = lax.all_to_all(by_channel, "blk", split_axis=0, concat_axis=1, tiled=True)
    turned = lax.all_to_all(by_block, "tch", split_axis=0, concat_axis=1, tiled=True)
    chan_local = turned.shape[0]
    layout = turned.reshape(chan_local, half_count, block_count, row_count, 2, spec_local)
    layout = jnp.transpose(layout, (0, 2, 3, 4, 1, 5))
    stacked = layout.reshape(chan_local, block_count * row_count, 2 * spec_total)
    ordered = reorder_inputs(stacked, station_of_slot, station_ok)
    inverse_count = 1.0 / spec_total
    return correlate_full(ordered, inverse_count)


def solution(mesh):
    return jax.shard_map(
        local,
        mesh=mesh,
        in_specs=(P("grp", "blk", "tch"), P("grp", "blk", None), P(), P("grp"), P("grp")),
        out_specs=P("grp", ("blk", "tch"), None, None),
        check_vma=False,
    )
```

profile of v0, /device:TPU:0, one launch (start us, length us, event | category | flops | bytes accessed | tf_op | source)
XLA Modules:
  0.0 76.3 jit_solution(1272274682949165277)
XLA Ops:
  0.0 1.0 %slice.106 = bf16[2,4,15360]{2,1,0:T(4,128)(2,1)S(1)} slice(bf16[2,4,32768]{2,1,0:T(4,128)(2,1)} %param.5), slice={[0:2], [0:4], [17408:32768]} | slice | bytes 491520 | tf_op jit(solution)/shard_map/slice | solution.py:84
  1.0 2.4 %collective-permute-start = (bf16[2,4,15360]{2,1,0:T(4,128)(2,1)S(1)}, bf16[2,4,15360]{2,1,0:T(4,128)(2,1)S(1)}, u32[]{:S(2)}, u32[]{:S(2)}) collective-permute-start(bf16[2,4,15360]{2,1,0:T(4,128)(2,1)S(1)} %slice.106), channel_id=1, source_target_pairs={{0,1},{2,3},{4,5},{6,7},{8,9},{10,11},{12,13},{14,15},{16,17},{18,... | collective-permute-start | bytes 737288 | tf_op jit(solution)/shard_map/ppermute | solution.py:13
  3.4 17.9 %negate_convert_fusion = (bf16[1024,1024]{1,0:T(8,128)(2,1)}, bf16[1024,1024]{1,0:T(8,128)(2,1)}) fusion(), kind=kLoop, calls=%fused_computation.18 | loop fusion | flops 19922944 | bytes 4194304 | tf_op jit(solution)/shard_map/convert.5
  21.4 16.6 %fusion.14 = bf16[1024,1024]{1,0:T(8,128)(2,1)} fusion(), kind=kLoop, calls=%fused_computation.24 | loop fusion | flops 16777216 | bytes 2097152 | tf_op jit(solution)/shard_map/convert.2
  38.1 0.3 pad_maximum_fusion
  38.4 0.5 reshape.130
  38.9 2.2 %fusion.25 = bf16[4,32,2,1024]{3,1,0,2:T(8,128)(2,1)S(1)} fusion(bf16[2,4,47,1024]{3,2,1,0:T(8,128)(2,1)S(1)} %reshape.130, f32[1024]{0:T(1024)S(1)} %bitcast.78, f32[1024]{0:T(1024)S(1)} %bitcast.79, f32[1024]{0:T(1024)S(1)} %bitcast.65, f32[1024]{0:T(1024)S(1)} %bitcast.66, f32[1024]{0:T(1024)S(1)} %bitcast.67, f32[1024]{0:T(1024)S(1)} %bitcast.68, ...), kind=kLoop, calls=%fused_computation.38 | loop fusion | flops 12582912 | bytes 8978432 | tf_op jit(solution)/shard_map/transpose | solution.py:42
  41.2 0.5 copy.24
  41.7 0.1 copy.34
  41.9 0.9 %copy-done.1 = bf16[1024,1024]{1,0:T(8,128)(2,1)S(1)} copy-done((bf16[1024,1024]{1,0:T(8,128)(2,1)S(1)}, bf16[1024,1024]{1,0:T(8,128)(2,1)}, u32[]{:S(2)}) %copy-start.1) | copy-done | bytes 2097176
  42.7 1.3 %fusion.15 = bf16[128,2048]{1,0:T(8,128)(2,1)S(1)} fusion(bf16[128,2048]{1,0:T(8,128)(2,1)S(1)} %bitcast.61, bf16[1024,1024]{1,0:T(8,128)(2,1)S(1)} %copy-done.2, bf16[1024,1024]{1,0:T(8,128)(2,1)S(1)} %copy-done.3, bf16[1024,1024]{1,0:T(8,128)(2,1)S(1)} %copy-done.1), kind=kOutput, calls=%fused_computation.25 | convolution fusion | flops 1107558400 | bytes 7340032 | tf_op jit(solution)/shard_map/dot_general | solution.py:43
  44.0 0.4 reshape.132
  44.6 0.9 %copy.26 = bf16[8,128,256]{1,2,0:T(8,128)(2,1)} copy(bf16[8,128,256]{1,0,2:T(8,128)(2,1)S(1)} %bitcast.59) | data formatting | bytes 1048576 | tf_op jit(solution)/shard_map/all_to_all | solution.py:90
  45.5 6.6 %all-to-all-start = ((bf16[8,128,256]{1,2,0:T(8,128)(2,1)}), bf16[8,128,256]{1,2,0:T(8,128)(2,1)S(1)}, u32[]{:S(2)}, u32[]{:S(2)}) async-start(bf16[8,128,256]{1,2,0:T(8,128)(2,1)} %copy.26), calls=%async_computation | async-start | bytes 1048576 | tf_op jit(solution)/shard_map/all_to_all | solution.py:90
  52.2 0.6 scatter_custom_fusion
  52.8 0.7 gather_fusion
  53.5 0.7 gather_fusion.2
  54.3 11.9 %all-to-all-done = bf16[8,128,256]{1,2,0:T(8,128)(2,1)S(1)} async-done(((bf16[8,128,256]{1,2,0:T(8,128)(2,1)}), bf16[8,128,256]{1,2,0:T(8,128)(2,1)S(1)}, u32[]{:S(2)}, u32[]{:S(2)}) %all-to-all-start) | async-done | bytes 524320 | tf_op jit(solution)/shard_map/all_to_all | solution.py:90
  66.2 0.4 copy.27
  66.6 0.2 all_to_all.27
  66.9 4.2 %all_to_all.32 = bf16[2,64,2048]{2,1,0:T(8,128)(2,1)S(1)} all-to-all(bf16[2,64,2048]{2,1,0:T(8,128)(2,1)S(1)} %all_to_all.27), channel_id=1, replica_groups=mesh['grp'=2,'blk'=8,'tch'=2] {'tch'}, dimensions={0} | all-to-all | bytes 1048576 | tf_op jit(solution)/shard_map/all_to_all | solution.py:91
  71.0 0.5 copy.28
  71.5 0.1 copy.29
  71.7 0.4 copy.30
  72.1 0.7 gather_fusion.1
  72.8 0.3 fusion.24
  73.1 0.2 slice_negate_fusion
  73.4 0.4 fusion.35
  73.7 0.5 fusion.19
  74.2 0.6 copy.33
  74.8 0.6 copy.32
  75.4 0.9 %fusion.18 = bf16[2,64,32,32]{1,3,2,0:T(8,128)(2,1)} fusion(f32[1,64,32,32]{1,3,2,0:T(8,128)S(1)} %bitcast.53, f32[1,64,32,32]{1,3,2,0:T(8,128)S(1)} %bitcast.54), kind=kLoop, calls=%fused_computation.27 | loop fusion | flops 393216 | bytes 786432 | tf_op jit(solution)/shard_map/convert_element_type | solution.py:73
  (28 shorter events, 0.4 us)
Async XLA Ops:
  0.0 53.5 %copy-start = (s32[16]{0:T(128)S(1)}, s32[16]{0:T(128)}, u32[]{:S(2)}) copy-start(s32[16]{0:T(128)} %param.9) | copy-start | bytes 196
  1.0 36.9 %collective-permute-start = (bf16[2,4,15360]{2,1,0:T(4,128)(2,1)S(1)}, bf16[2,4,15360]{2,1,0:T(4,128)(2,1)S(1)}, u32[]{:S(2)}, u32[]{:S(2)}) collective-permute-start(bf16[2,4,15360]{2,1,0:T(4,128)(2,1)S(1)} %slice.106), channel_id=1, source_target_pairs={{0,1},{2,3},{4,5},{6,7},{8,9},{10,11},{12,13},{14,15},{16,17},{18,... | collective-permute-start | bytes 737288 | tf_op jit(solution)/shard_map/ppermute | solution.py:13
  21.4 16.6 %copy-start.6 = (f32[16,1024]{1,0:T(8,128)S(1)}, f32[16,1024]{1,0:T(8,128)}, u32[]{:S(2)}) copy-start(f32[16,1024]{1,0:T(8,128)} %param.7) | copy-start | bytes 196612
  21.4 16.6 %copy-start.5 = (bf16[2,4,15360]{2,1,0:T(4,128)(2,1)S(1)}, bf16[2,4,15360]{2,1,0:T(4,128)(2,1)}, u32[]{:S(2)}) copy-start(bf16[2,4,15360]{2,1,0:T(4,128)(2,1)} %param.6) | copy-start | bytes 737284
  21.4 16.7 %copy-start.4 = (bf16[2,4,32768]{2,1,0:T(4,128)(2,1)S(1)}, bf16[2,4,32768]{2,1,0:T(4,128)(2,1)}, u32[]{:S(2)}) copy-start(bf16[2,4,32768]{2,1,0:T(4,128)(2,1)} %param.5) | copy-start | bytes 1572868
  38.9 2.9 %copy-start.2 = (bf16[1024,1024]{1,0:T(8,128)(2,1)S(1)}, bf16[1024,1024]{1,0:T(8,128)(2,1)}, u32[]{:S(2)}) copy-start(bf16[1024,1024]{1,0:T(8,128)(2,1)} %get-tuple-element.24) | copy-start | bytes 6291460
  38.9 2.9 %copy-start.3 = (bf16[1024,1024]{1,0:T(8,128)(2,1)S(1)}, bf16[1024,1024]{1,0:T(8,128)(2,1)}, u32[]{:S(2)}) copy-start(bf16[1024,1024]{1,0:T(8,128)(2,1)} %fusion.14) | copy-start | bytes 6291460
  41.2 1.6 %copy-start.1 = (bf16[1024,1024]{1,0:T(8,128)(2,1)S(1)}, bf16[1024,1024]{1,0:T(8,128)(2,1)}, u32[]{:S(2)}) copy-start(bf16[1024,1024]{1,0:T(8,128)(2,1)} %get-tuple-element.23) | copy-start | bytes 6291460
  44.4 7.8 %copy-start.7 = (s32[16]{0:T(128)S(1)}, s32[16]{0:T(128)}, u32[]{:S(2)}) copy-start(s32[16]{0:T(128)} %param.8) | copy-start | bytes 196
  45.5 20.7 %all-to-all-start = ((bf16[8,128,256]{1,2,0:T(8,128)(2,1)}), bf16[8,128,256]{1,2,0:T(8,128)(2,1)S(1)}, u32[]{:S(2)}, u32[]{:S(2)}) async-start(bf16[8,128,256]{1,2,0:T(8,128)(2,1)} %copy.26), calls=%async_computation | async-start | bytes 1048576 | tf_op jit(solution)/shard_map/all_to_all | solution.py:90
where the time goes:
time: 76.6 us; the launch traced here: 76.3 us
  other arithmetic  38.6 us (50%)
  waiting for transfers between devices  11.9 us (16%)
  local copies, waits for them, and re-layouts  10.2 us (13%)
  starting transfers between devices  9 us (12%)
  blocking collectives  4.15 us (5%)
  matrix products  2.12 us (3%)
    another operation x2, other arithmetic  34.5 us
    all_to_all x1, waiting for transfers between devices, local(): lax.all_to_all(by_channel, 'blk', split_axis=0, concat_axis=1, tiled=True)  11.9 us
    all_to_all x1, starting transfers between devices, local(): lax.all_to_all(by_channel, 'blk', split_axis=0, concat_axis=1, tiled=True)  6.63 us
    all_to_all x1, blocking collectives, local(): lax.all_to_all(by_block, 'tch', split_axis=0, concat_axis=1, tiled=True)  4.15 us
    ppermute x1, starting transfers between devices, shifted(): return lax.ppermute(block, axis, route)  2.37 us
    transpose x1, other arithmetic, channel_major(): jnp.transpose(filtered, (1, 2, 0, 3))  2.23 us
  transfers between devices with their start and end apart: 2, of which 1 were waited for; matrix products, arithmetic and copies ran while one was open for 48% of the time, Pallas kernels for 0%

commit v1 on v0

--- a/solution.py
+++ b/solution.py
@@ -5,6 +5,17 @@
 from jax.sharding import PartitionSpec as P
 
 POLS = 2
+
+
+def in_blocks(array, dim, count):
+    before, after = (array.shape[:dim], array.shape[dim + 1 :])
+    return jnp.moveaxis(array.reshape(*before, count, -1, *after), dim, 0)
+
+
+def laid_out(blocks, dim):
+    blocks = jnp.moveaxis(blocks, 0, dim)
+    shape = blocks.shape
+    return blocks.reshape(*shape[:dim], shape[dim] * shape[dim + 1], *shape[dim + 2 :])
 
 
 def shifted(block, axis, distance):
@@ -87,7 +98,17 @@
     earlier = jnp.where(is_first, history, earlier)
     extended = jnp.concatenate([earlier, samples], axis=2)
     by_channel = channel_major(filter_bank(extended, coefficients, spec_local), dft_matrix)
-    by_block = lax.all_to_all(by_channel, "blk", split_axis=0, concat_axis=1, tiled=True)
+    devices_2, here = (lax.axis_size("blk"), lax.axis_index("blk"))
+    blocks_2 = in_blocks(by_channel, 0, devices_2)
+    whole = blocks_2
+    for hop in range(1, devices_2):
+        target, source = ((here + hop) % devices_2, (here - hop) % devices_2)
+        sent = lax.dynamic_index_in_dim(blocks_2, target, 0)
+        partner_block = lax.ppermute(
+            sent, "blk", [(i_2, (i_2 + hop) % devices_2) for i_2 in range(devices_2)]
+        )
+        whole = lax.dynamic_update_slice_in_dim(whole, partner_block, source, axis=0)
+    by_block = laid_out(whole, 1)
     turned = lax.all_to_all(by_block, "tch", split_axis=0, concat_axis=1, tiled=True)
     chan_local = turned.shape[0]
     layout = turned.reshape(chan_local, half_count, block_count, row_count, 2, spec_local)

time: 76.6 us -> 99 us (1.29)
  the two profiles are of different devices: /device:TPU:0 before, /device:TPU:25 now
where the time goes in v1:
time: 99 us; the launch traced here: 98.8 us
  other arithmetic  38.6 us (39%)
  local copies, waits for them, and re-layouts  30.2 us (31%)
  blocking collectives  11.2 us (11%)
  starting transfers between devices  8.48 us (9%)
  waiting for transfers between devices  7.53 us (8%)
  matrix products  2.12 us (2%)
    another operation x2, other arithmetic  34.5 us
    dynamic_update_slice x7, local copies, waits for them, and re-layouts, local(): lax.dynamic_update_slice_in_dim(whole, partner_block, source, axis=0)  19.7 us
    all_to_all x1, blocking collectives, local(): lax.all_to_all(by_block, 'tch', split_axis=0, concat_axis=1, tiled=True)  11.2 us
    ppermute x7, waiting for transfers between devices, local(): lax.ppermute(sent, 'blk', [(i_2, (i_2 + hop) % devices_2) for i_2 in rang...  7.53 us
    ppermute x7, starting transfers between devices, local(): lax.ppermute(sent, 'blk', [(i_2, (i_2 + hop) % devices_2) for i_2 in rang...  7.18 us
    transpose x1, other arithmetic, channel_major(): jnp.transpose(filtered, (1, 2, 0, 3))  2.23 us
  transfers between devices with their start and end apart: 8, of which 1 were waited for; matrix products, arithmetic and copies ran while one was open for 54% of the time, Pallas kernels for 0%

profile of v1, /device:TPU:25, one launch (start us, length us, event | category | flops | bytes accessed | tf_op | source)
XLA Modules:
  0.0 98.8 jit_solution(910680242159001023)
XLA Ops:
  0.0 1.0 %slice.106 = bf16[2,4,15360]{2,1,0:T(4,128)(2,1)S(1)} slice(bf16[2,4,32768]{2,1,0:T(4,128)(2,1)} %param.5), slice={[0:2], [0:4], [17408:32768]} | slice | bytes 491520 | tf_op jit(solution)/shard_map/slice | solution.py:95
  1.0 1.3 %collective-permute-start = (bf16[2,4,15360]{2,1,0:T(4,128)(2,1)S(1)}, bf16[2,4,15360]{2,1,0:T(4,128)(2,1)S(1)}, u32[]{:S(2)}, u32[]{:S(2)}) collective-permute-start(bf16[2,4,15360]{2,1,0:T(4,128)(2,1)S(1)} %slice.106), channel_id=1, source_target_pairs={{0,1},{2,3},{4,5},{6,7},{8,9},{10,11},{12,13},{14,15},{16,17},{18,... | collective-permute-start | bytes 737288 | tf_op jit(solution)/shard_map/ppermute | solution.py:24
  2.3 17.9 %negate_convert_fusion = (bf16[1024,1024]{1,0:T(8,128)(2,1)}, bf16[1024,1024]{1,0:T(8,128)(2,1)}) fusion(), kind=kLoop, calls=%fused_computation.18 | loop fusion | flops 19922944 | bytes 4194304 | tf_op jit(solution)/shard_map/convert.5
  20.3 16.6 %fusion.14 = bf16[1024,1024]{1,0:T(8,128)(2,1)} fusion(), kind=kLoop, calls=%fused_computation.24 | loop fusion | flops 16777216 | bytes 2097152 | tf_op jit(solution)/shard_map/convert.2
  36.9 0.6 scatter_custom_fusion
  37.6 0.7 gather_fusion
  38.8 0.5 reshape.126
  39.4 2.2 %fusion.25 = bf16[4,32,2,1024]{3,1,0,2:T(8,128)(2,1)S(1)} fusion(bf16[2,4,47,1024]{3,2,1,0:T(8,128)(2,1)S(1)} %reshape.126, f32[1024]{0:T(1024)S(1)} %bitcast.79, f32[1024]{0:T(1024)S(1)} %bitcast.80, f32[1024]{0:T(1024)S(1)} %bitcast.66, f32[1024]{0:T(1024)S(1)} %bitcast.67, f32[1024]{0:T(1024)S(1)} %bitcast.68, f32[1024]{0:T(1024)S(1)} %bitcast.69, ...), kind=kLoop, calls=%fused_computation.38 | loop fusion | flops 12582912 | bytes 8978432 | tf_op jit(solution)/shard_map/transpose | solution.py:53
  41.6 0.5 copy.15
  42.3 0.9 copy-done.1
  43.2 1.3 %fusion.15 = bf16[128,2048]{1,0:T(8,128)(2,1)S(1)} fusion(bf16[128,2048]{1,0:T(8,128)(2,1)S(1)} %bitcast.62, bf16[1024,1024]{1,0:T(8,128)(2,1)S(1)} %copy-done.2, bf16[1024,1024]{1,0:T(8,128)(2,1)S(1)} %copy-done.3, bf16[1024,1024]{1,0:T(8,128)(2,1)S(1)} %copy-done.1), kind=kOutput, calls=%fused_computation.25 | convolution fusion | flops 1107558400 | bytes 7340032 | tf_op jit(solution)/shard_map/dot_general | solution.py:54
  45.1 1.0 constant_dynamic-slice_fusion
  46.0 1.3 %collective-permute-start.1 = (bf16[1,128,256]{1,0,2:T(2,128)(2,1)S(1)}, bf16[1,128,256]{1,0,2:T(2,128)(2,1)S(1)}, u32[]{:S(2)}, u32[]{:S(2)}) collective-permute-start(bf16[1,128,256]{1,0,2:T(2,128)(2,1)S(1)} %get-tuple-element.13), channel_id=1, source_target_pairs={{0,2},{2,4},{4,6},{6,8},{8,10},{10,12},{12,14},{14,0},{1,3},{3,5},... | collective-permute-start | bytes 196616 | tf_op jit(solution)/shard_map/ppermute | solution.py:107
  47.4 0.7 gather_fusion.2
  48.2 2.1 %collective-permute-start.3 = (bf16[1,128,256]{1,0,2:T(2,128)(2,1)S(1)}, bf16[1,128,256]{1,0,2:T(2,128)(2,1)S(1)}, u32[]{:S(2)}, u32[]{:S(2)}) collective-permute-start(bf16[1,128,256]{1,0,2:T(2,128)(2,1)S(1)} %get-tuple-element.11), channel_id=1, source_target_pairs={{0,6},{2,8},{4,10},{6,12},{8,14},{10,0},{12,2},{14,4},{1,7},{3,9},... | collective-permute-start | bytes 196616 | tf_op jit(solution)/shard_map/ppermute | solution.py:107
  50.6 2.1 %collective-permute-start.5 = (bf16[1,128,256]{1,0,2:T(2,128)(2,1)S(1)}, bf16[1,128,256]{1,0,2:T(2,128)(2,1)S(1)}, u32[]{:S(2)}, u32[]{:S(2)}) collective-permute-start(bf16[1,128,256]{1,0,2:T(2,128)(2,1)S(1)} %get-tuple-element.9), channel_id=1, source_target_pairs={{0,10},{2,12},{4,14},{6,0},{8,2},{10,4},{12,6},{14,8},{1,11},{3,13... | collective-permute-start | bytes 196616 | tf_op jit(solution)/shard_map/ppermute | solution.py:107
  52.9 1.2 %collective-permute-start.7 = (bf16[1,128,256]{1,0,2:T(2,128)(2,1)S(1)}, bf16[1,128,256]{1,0,2:T(2,128)(2,1)S(1)}, u32[]{:S(2)}, u32[]{:S(2)}) collective-permute-start(bf16[1,128,256]{1,0,2:T(2,128)(2,1)S(1)} %get-tuple-element.7), channel_id=1, source_target_pairs={{0,14},{2,0},{4,2},{6,4},{8,6},{10,8},{12,10},{14,12},{1,15},{3,1}... | collective-permute-start | bytes 196616 | tf_op jit(solution)/shard_map/ppermute | solution.py:107
  54.1 2.8 %dynamic_update_slice.21 = bf16[8,128,256]{1,0,2:T(8,128)(2,1)S(1)} dynamic-update-slice(bf16[8,128,256]{1,0,2:T(8,128)(2,1)S(1)} %bitcast.52, bf16[1,128,256]{1,0,2:T(2,128)(2,1)S(1)} %collective-permute-done.1, s32[]{:T(128)S(6)} %select_n.200, s32[]{:T(128)} %constant.160.clone.1, s32[]{:T(128)} %constant.160.clone.1) | dynamic-update-slice | bytes 131076 | tf_op jit(solution)/shard_map/dynamic_update_slice | solution.py:110
  56.9 2.8 %dynamic_update_slice.22 = bf16[8,128,256]{1,0,2:T(8,128)(2,1)S(1)} dynamic-update-slice(bf16[8,128,256]{1,0,2:T(8,128)(2,1)S(1)} %dynamic_update_slice.21, bf16[1,128,256]{1,0,2:T(2,128)(2,1)S(1)} %collective-permute-done.2, s32[]{:T(128)S(6)} %select_n.204, s32[]{:T(128)} %constant.160.clone.1, s32[]{:T(128)} %constant.160.clone.1) | dynamic-update-slice | bytes 131076 | tf_op jit(solution)/shard_map/dynamic_update_slice | solution.py:110
  59.8 7.5 %collective-permute-done.3 = bf16[1,128,256]{1,0,2:T(2,128)(2,1)S(1)} collective-permute-done((bf16[1,128,256]{1,0,2:T(2,128)(2,1)S(1)}, bf16[1,128,256]{1,0,2:T(2,128)(2,1)S(1)}, u32[]{:S(2)}, u32[]{:S(2)}) %collective-permute-start.3) | collective-permute-done | bytes 65568 | tf_op jit(solution)/shard_map/ppermute | solution.py:107
  67.3 2.8 %dynamic_update_slice.23 = bf16[8,128,256]{1,0,2:T(8,128)(2,1)S(1)} dynamic-update-slice(bf16[8,128,256]{1,0,2:T(8,128)(2,1)S(1)} %dynamic_update_slice.22, bf16[1,128,256]{1,0,2:T(2,128)(2,1)S(1)} %collective-permute-done.3, s32[]{:T(128)S(6)} %select_n.208, s32[]{:T(128)} %constant.160.clone.1, s32[]{:T(128)} %constant.160.clone.1) | dynamic-update-slice | bytes 131076 | tf_op jit(solution)/shard_map/dynamic_update_slice | solution.py:110
  70.1 2.8 %dynamic_update_slice.24 = bf16[8,128,256]{1,0,2:T(8,128)(2,1)S(1)} dynamic-update-slice(bf16[8,128,256]{1,0,2:T(8,128)(2,1)S(1)} %dynamic_update_slice.23, bf16[1,128,256]{1,0,2:T(2,128)(2,1)S(1)} %collective-permute-done.4, s32[]{:T(128)S(6)} %select_n.212, s32[]{:T(128)} %constant.160.clone.1, s32[]{:T(128)} %constant.160.clone.1) | dynamic-update-slice | bytes 131076 | tf_op jit(solution)/shard_map/dynamic_update_slice | solution.py:110
  72.9 2.8 %dynamic_update_slice.25 = bf16[8,128,256]{1,0,2:T(8,128)(2,1)S(1)} dynamic-update-slice(bf16[8,128,256]{1,0,2:T(8,128)(2,1)S(1)} %dynamic_update_slice.24, bf16[1,128,256]{1,0,2:T(2,128)(2,1)S(1)} %collective-permute-done.5, s32[]{:T(128)S(6)} %select_n.216, s32[]{:T(128)} %constant.160.clone.1, s32[]{:T(128)} %constant.160.clone.1) | dynamic-update-slice | bytes 131076 | tf_op jit(solution)/shard_map/dynamic_update_slice | solution.py:110
  75.8 2.8 %dynamic_update_slice.26 = bf16[8,128,256]{1,0,2:T(8,128)(2,1)S(1)} dynamic-update-slice(bf16[8,128,256]{1,0,2:T(8,128)(2,1)S(1)} %dynamic_update_slice.25, bf16[1,128,256]{1,0,2:T(2,128)(2,1)S(1)} %collective-permute-done.6, s32[]{:T(128)S(6)} %select_n.220, s32[]{:T(128)} %constant.160.clone.1, s32[]{:T(128)} %constant.160.clone.1) | dynamic-update-slice | bytes 131076 | tf_op jit(solution)/shard_map/dynamic_update_slice | solution.py:110
  78.6 2.8 %dynamic_update_slice.27 = bf16[8,128,256]{1,0,2:T(8,128)(2,1)S(1)} dynamic-update-slice(bf16[8,128,256]{1,0,2:T(8,128)(2,1)S(1)} %dynamic_update_slice.26, bf16[1,128,256]{1,0,2:T(2,128)(2,1)S(1)} %collective-permute-done.7, s32[]{:T(128)S(6)} %select_n.224, s32[]{:T(128)} %constant.160.clone.1, s32[]{:T(128)} %constant.160.clone.1) | dynamic-update-slice | bytes 131076 | tf_op jit(solution)/shard_map/dynamic_update_slice | solution.py:110
  81.4 0.6 copy.17
  82.3 11.2 %all_to_all.16 = bf16[2,64,2048]{2,1,0:T(8,128)(2,1)S(1)} all-to-all(bf16[2,64,2048]{2,1,0:T(8,128)(2,1)S(1)} %all_to_all.12), channel_id=1, replica_groups=mesh['grp'=2,'blk'=8,'tch'=2] {'tch'}, dimensions={0} | all-to-all | bytes 1048576 | tf_op jit(solution)/shard_map/all_to_all | solution.py:112
  93.5 0.5 copy.18
  94.6 0.7 gather_fusion.1
  96.7 0.6 copy.23
  97.3 0.6 copy.22
  97.9 0.9 fusion.18
  (47 shorter events, 3.9 us)
Async XLA Ops:
  0.0 47.4 %copy-start = (s32[16]{0:T(128)S(1)}, s32[16]{0:T(128)}, u32[]{:S(2)}) copy-start(s32[16]{0:T(128)} %param.9) | copy-start | bytes 196
  1.0 37.4 %collective-permute-start = (bf16[2,4,15360]{2,1,0:T(4,128)(2,1)S(1)}, bf16[2,4,15360]{2,1,0:T(4,128)(2,1)S(1)}, u32[]{:S(2)}, u32[]{:S(2)}) collective-permute-start(bf16[2,4,15360]{2,1,0:T(4,128)(2,1)S(1)} %slice.106), channel_id=1, source_target_pairs={{0,1},{2,3},{4,5},{6,7},{8,9},{10,11},{12,13},{14,15},{16,17},{18,... | collective-permute-start | bytes 737288 | tf_op jit(solution)/shard_map/ppermute | solution.py:24
  20.3 16.6 %copy-start.7 = (s32[16]{0:T(128)S(1)}, s32[16]{0:T(128)}, u32[]{:S(2)}) copy-start(s32[16]{0:T(128)} %param.8) | copy-start | bytes 196
  20.3 18.1 %copy-start.6 = (f32[16,1024]{1,0:T(8,128)S(1)}, f32[16,1024]{1,0:T(8,128)}, u32[]{:S(2)}) copy-start(f32[16,1024]{1,0:T(8,128)} %param.7) | copy-start | bytes 196612
  20.3 18.1 %copy-start.5 = (bf16[2,4,15360]{2,1,0:T(4,128)(2,1)S(1)}, bf16[2,4,15360]{2,1,0:T(4,128)(2,1)}, u32[]{:S(2)}) copy-start(bf16[2,4,15360]{2,1,0:T(4,128)(2,1)} %param.6) | copy-start | bytes 737284
  20.3 18.2 %copy-start.4 = (bf16[2,4,32768]{2,1,0:T(4,128)(2,1)S(1)}, bf16[2,4,32768]{2,1,0:T(4,128)(2,1)}, u32[]{:S(2)}) copy-start(bf16[2,4,32768]{2,1,0:T(4,128)(2,1)} %param.5) | copy-start | bytes 1572868
  39.3 2.9 %copy-start.2 = (bf16[1024,1024]{1,0:T(8,128)(2,1)S(1)}, bf16[1024,1024]{1,0:T(8,128)(2,1)}, u32[]{:S(2)}) copy-start(bf16[1024,1024]{1,0:T(8,128)(2,1)} %get-tuple-element.31) | copy-start | bytes 6291460
  39.4 2.9 %copy-start.3 = (bf16[1024,1024]{1,0:T(8,128)(2,1)S(1)}, bf16[1024,1024]{1,0:T(8,128)(2,1)}, u32[]{:S(2)}) copy-start(bf16[1024,1024]{1,0:T(8,128)(2,1)} %fusion.14) | copy-start | bytes 6291460
  41.6 1.6 %copy-start.1 = (bf16[1024,1024]{1,0:T(8,128)(2,1)S(1)}, bf16[1024,1024]{1,0:T(8,128)(2,1)}, u32[]{:S(2)}) copy-start(bf16[1024,1024]{1,0:T(8,128)(2,1)} %get-tuple-element.30) | copy-start | bytes 6291460
  46.0 6.7 %collective-permute-start.1 = (bf16[1,128,256]{1,0,2:T(2,128)(2,1)S(1)}, bf16[1,128,256]{1,0,2:T(2,128)(2,1)S(1)}, u32[]{:S(2)}, u32[]{:S(2)}) collective-permute-start(bf16[1,128,256]{1,0,2:T(2,128)(2,1)S(1)} %get-tuple-element.13), channel_id=1, source_target_pairs={{0,2},{2,4},{4,6},{6,8},{8,10},{10,12},{12,14},{14,0},{1,3},{3,5},... | collective-permute-start | bytes 196616 | tf_op jit(solution)/shard_map/ppermute | solution.py:107
  47.3 5.6 %collective-permute-start.2 = (bf16[1,128,256]{1,0,2:T(2,128)(2,1)S(1)}, bf16[1,128,256]{1,0,2:T(2,128)(2,1)S(1)}, u32[]{:S(2)}, u32[]{:S(2)}) collective-permute-start(bf16[1,128,256]{1,0,2:T(2,128)(2,1)S(1)} %get-tuple-element.12), channel_id=1, source_target_pairs={{0,4},{2,6},{4,8},{6,10},{8,12},{10,14},{12,0},{14,2},{1,5},{3,7},... | collective-permute-start | bytes 196616 | tf_op jit(solution)/shard_map/ppermute | solution.py:107
  48.2 19.1 %collective-permute-start.3 = (bf16[1,128,256]{1,0,2:T(2,128)(2,1)S(1)}, bf16[1,128,256]{1,0,2:T(2,128)(2,1)S(1)}, u32[]{:S(2)}, u32[]{:S(2)}) collective-permute-start(bf16[1,128,256]{1,0,2:T(2,128)(2,1)S(1)} %get-tuple-element.11), channel_id=1, source_target_pairs={{0,6},{2,8},{4,10},{6,12},{8,14},{10,0},{12,2},{14,4},{1,7},{3,9},... | collective-permute-start | bytes 196616 | tf_op jit(solution)/shard_map/ppermute | solution.py:107
  50.3 19.8 %collective-permute-start.4 = (bf16[1,128,256]{1,0,2:T(2,128)(2,1)S(1)}, bf16[1,128,256]{1,0,2:T(2,128)(2,1)S(1)}, u32[]{:S(2)}, u32[]{:S(2)}) collective-permute-start(bf16[1,128,256]{1,0,2:T(2,128)(2,1)S(1)} %get-tuple-element.10), channel_id=1, source_target_pairs={{0,8},{2,10},{4,12},{6,14},{8,0},{10,2},{12,4},{14,6},{1,9},{3,11}... | collective-permute-start | bytes 196616 | tf_op jit(solution)/shard_map/ppermute | solution.py:107
  50.6 22.3 %collective-permute-start.5 = (bf16[1,128,256]{1,0,2:T(2,128)(2,1)S(1)}, bf16[1,128,256]{1,0,2:T(2,128)(2,1)S(1)}, u32[]{:S(2)}, u32[]{:S(2)}) collective-permute-start(bf16[1,128,256]{1,0,2:T(2,128)(2,1)S(1)} %get-tuple-element.9), channel_id=1, source_target_pairs={{0,10},{2,12},{4,14},{6,0},{8,2},{10,4},{12,6},{14,8},{1,11},{3,13... | collective-permute-start | bytes 196616 | tf_op jit(solution)/shard_map/ppermute | solution.py:107
  52.7 23.0 %collective-permute-start.6 = (bf16[1,128,256]{1,0,2:T(2,128)(2,1)S(1)}, bf16[1,128,256]{1,0,2:T(2,128)(2,1)S(1)}, u32[]{:S(2)}, u32[]{:S(2)}) collective-permute-start(bf16[1,128,256]{1,0,2:T(2,128)(2,1)S(1)} %get-tuple-element.8), channel_id=1, source_target_pairs={{0,12},{2,14},{4,0},{6,2},{8,4},{10,6},{12,8},{14,10},{1,13},{3,15... | collective-permute-start | bytes 196616 | tf_op jit(solution)/shard_map/ppermute | solution.py:107
  52.9 25.7 %collective-permute-start.7 = (bf16[1,128,256]{1,0,2:T(2,128)(2,1)S(1)}, bf16[1,128,256]{1,0,2:T(2,128)(2,1)S(1)}, u32[]{:S(2)}, u32[]{:S(2)}) collective-permute-start(bf16[1,128,256]{1,0,2:T(2,128)(2,1)S(1)} %get-tuple-element.7), channel_id=1, source_target_pairs={{0,14},{2,0},{4,2},{6,4},{8,6},{10,8},{12,10},{14,12},{1,15},{3,1}... | collective-permute-start | bytes 196616 | tf_op jit(solution)/shard_map/ppermute | solution.py:107
